TPU v7x, 32 devices: a whole 2x2x4 slice. The times are simulated.
32 devices in a mesh: groups: 2 (over x), chan: 16 (over z, y, core).
Axes of the slice: x: 2, y: 2, z: 4, core: 2. Of those that a mesh axis runs over, the one named last changes fastest.
Arguments:
- traces: float32 [2048, 1152], P(('groups', 'chan')), parts along dimension 0, as said below
- good_mask: int32 [2048], P(('groups', 'chan')), parts along dimension 0, may hold values 0 or 1
Outputs:
- correlations: bfloat16 [2048, 64, 1024], P(('groups', 'chan')), parts along dimension 0
There are 2 independent parts, one for each index of `groups`. A program takes and returns all parts, laid end to end along the dimension named above; each array names one. Nothing has to cross between parts.
Inputs may be any that keep to these rules, and one draw needn't show every extreme that they name: `traces`: traces of order one.
All inputs are finite; a program needn't handle non-finite values. No bound on the sum of `good_mask` on one device may be relied on, other than what follows from the above.
Results may differ from a plain program's by a relative error of at most 0.0053.
Values may be sent and summed in bfloat16 or wider, within the bound.
No kernel may reach another device: no remote copies, remote signals or barrier semaphores. Data moves between devices by JAX's collectives and lax.ppermute only.
A program may use at most 128 MiB of HBM per device.

v0:
```python
import math
import jax
import jax.numpy as jnp
from jax import lax
from jax.sharding import PartitionSpec as P

NW = 256
NF = 128
HOP = 128
LAGS = 64
NWIN = 8


def spread(value, axis, root):
    mine = lax.axis_index(axis) == root
    return lax.psum(jnp.where(mine, value, jnp.zeros_like(value)), axis)


def forward_table(width, bins):
    samples = jnp.arange(width)
    freqs = jnp.arange(1, bins + 1)
    phase = samples[:, None] * freqs[None, :] % width
    theta = 2.0 * math.pi * phase.astype(jnp.float32) / width
    hann = 0.5 - 0.5 * jnp.cos(2.0 * math.pi * samples.astype(jnp.float32) / width)
    return jnp.concatenate(
        [hann[:, None] * jnp.cos(theta), -hann[:, None] * jnp.sin(theta)], axis=1
    )


def lag_table(width, bins, lag_count):
    freqs = jnp.arange(1, bins + 1)
    lags = jnp.arange(lag_count) - lag_count // 2
    phase = freqs[:, None] * lags[None, :] % width
    theta = 2.0 * math.pi * phase.astype(jnp.float32) / width
    return (jnp.concatenate([jnp.cos(theta), -jnp.sin(theta)], axis=0) / bins).astype(jnp.bfloat16)


def pair_block(own, other, table, windows):
    bins = own.shape[2] // 2
    own_real, own_imag = (own[..., :bins], own[..., bins:])
    other_real, other_imag = (other[..., :bins], other[..., bins:])

    def product(left, right):
        return jnp.einsum("wif,wjf->ijf", left, right, preferred_element_type=jnp.float32)

    real_sum = product(own_real, other_real) + product(own_imag, other_imag)
    imag_sum = product(own_imag, other_real) - product(own_real, other_imag)
    stack = (jnp.concatenate([real_sum, imag_sum], axis=2) / windows).astype(jnp.bfloat16)
    result = jnp.einsum("ijk,kl->ilj", stack, table, preferred_element_type=jnp.float32)
    return result.astype(jnp.bfloat16)


def shards(traces, good_mask):
    channels_here = traces.shape[0]
    windows = NWIN
    good = good_mask.astype(jnp.float32)
    total, count = lax.psum((jnp.sum(traces * good[:, None], axis=0), jnp.sum(good)), "chan")
    common = total / jnp.maximum(count, 1.0)
    clean = (traces - common[None, :]) * good[:, None]
    halves = clean.reshape(channels_here, windows + 1, HOP)
    segments = jnp.concatenate([halves[:, :-1], halves[:, 1:]], axis=2)
    spectrum = jnp.einsum(
        "cwn,nk->wck", segments, forward_table(NW, NF), precision=lax.Precision.HIGHEST
    )
    real_part = spectrum[..., :NF]
    imag_part = spectrum[..., NF:]
    power = real_part * real_part + imag_part * imag_part
    magnitude = jnp.sqrt(power)
    level = jnp.sqrt(jnp.mean(power, axis=-1, keepdims=True) + 1e-06)
    denom = jnp.maximum(magnitude, 0.3 * level)
    whitened = jnp.concatenate([real_part / denom, imag_part / denom], axis=-1).astype(jnp.bfloat16)
    table = lag_table(NW, NF, LAGS)
    owners = lax.axis_size("chan")
    result = jnp.zeros((channels_here, LAGS, channels_here * owners), jnp.bfloat16)

    def visit(owner, current):
        other = spread(whitened, "chan", owner)
        block = pair_block(whitened, other, table, windows)
        start = (owner * channels_here).astype(jnp.int32)
        return lax.dynamic_update_slice(current, block, (jnp.int32(0), jnp.int32(0), start))

    result = lax.fori_loop(0, owners, visit, result)
    return result


def solution(mesh):
    placed = (P(("groups", "chan"), None), P(("groups", "chan")))
    return jax.shard_map(
        shards,
        mesh=mesh,
        in_specs=placed,
        out_specs=P(("groups", "chan"), None, None),
        check_vma=False,
    )
```

profile of v0, /device:TPU:0, one launch (start us, length us, event | category | flops | bytes accessed | tf_op | source)
XLA Modules:
  0.0 2380.2 jit_solution(5177793545426857006)
XLA Ops:
  9.5 36.6 %all-reduce = (f32[1152]{0:T(1024)S(1)}, f32[]{:T(128)}) all-reduce(f32[1152]{0:T(1024)S(1)} %multiply_reduce_fusion, f32[]{:T(128)} %convert_reduce_fusion), channel_id=1, replica_groups=mesh['groups'=2,'chan'=16] {'chan'}, use_global_device_ids=true, to_apply=%region_1.0 | all-reduce | flops 1153 | bytes 9224 | tf_op jit(solution)/shard_map/psum | solution.py:57
  54.4 2319.3 %while.13 = (s32[]{:T(128)}, bf16[64,64,1024]{2,1,0:T(8,128)(2,1)}, bf16[8,64,256]{2,1,0:T(8,128)(2,1)S(1)}, bf16[256,64]{0,1:T(8,128)(2,1)S(1)}, s32[]{:T(128)}...) while((s32[]{:T(128)}, bf16[64,64,1024]{2,1,0:T(8,128)(2,1)}, bf16[8,64,256]{2,1,0:T(8,128)(2,1)S(1)}, ...), condition=%wide.region_7.8_spmd, body=%wide.region_5.7_spmd.sunk | while | flops 172490752 | bytes 48791760 | solution.py:82
  55.6 90.0 %all-reduce.3.cloned.1.call-done = bf16[8,64,256]{2,1,0:T(8,128)(2,1)} async-done(((bf16[8,64,256]{2,1,0:T(8,128)(2,1)}), bf16[8,64,256]{2,1,0:T(8,128)(2,1)}) %all-reduce.3.cloned.1.call-update) | async-done | bytes 262160 | tf_op jit(solution)/shard_map/while/body/eval_jaxpr/psum | solution.py:16
  183.2 10.6 dynamic_update_slice.8
  195.0 93.3 %all-reduce.3.cloned.1.call-done = bf16[8,64,256]{2,1,0:T(8,128)(2,1)} async-done(((bf16[8,64,256]{2,1,0:T(8,128)(2,1)}), bf16[8,64,256]{2,1,0:T(8,128)(2,1)}) %all-reduce.3.cloned.1.call-update) | async-done | bytes 262160 | tf_op jit(solution)/shard_map/while/body/eval_jaxpr/psum | solution.py:16
  325.9 16.0 dynamic_update_slice.8
  343.2 93.3 %all-reduce.3.cloned.1.call-done = bf16[8,64,256]{2,1,0:T(8,128)(2,1)} async-done(((bf16[8,64,256]{2,1,0:T(8,128)(2,1)}), bf16[8,64,256]{2,1,0:T(8,128)(2,1)}) %all-reduce.3.cloned.1.call-update) | async-done | bytes 262160 | tf_op jit(solution)/shard_map/while/body/eval_jaxpr/psum | solution.py:16
  474.1 10.6 dynamic_update_slice.8
  485.8 92.9 %all-reduce.3.cloned.1.call-done = bf16[8,64,256]{2,1,0:T(8,128)(2,1)} async-done(((bf16[8,64,256]{2,1,0:T(8,128)(2,1)}), bf16[8,64,256]{2,1,0:T(8,128)(2,1)}) %all-reduce.3.cloned.1.call-update) | async-done | bytes 262160 | tf_op jit(solution)/shard_map/while/body/eval_jaxpr/psum | solution.py:16
  616.4 16.0 dynamic_update_slice.8
  633.7 92.9 %all-reduce.3.cloned.1.call-done = bf16[8,64,256]{2,1,0:T(8,128)(2,1)} async-done(((bf16[8,64,256]{2,1,0:T(8,128)(2,1)}), bf16[8,64,256]{2,1,0:T(8,128)(2,1)}) %all-reduce.3.cloned.1.call-update) | async-done | bytes 262160 | tf_op jit(solution)/shard_map/while/body/eval_jaxpr/psum | solution.py:16
  764.2 10.6 dynamic_update_slice.8
  776.0 92.9 %all-reduce.3.cloned.1.call-done = bf16[8,64,256]{2,1,0:T(8,128)(2,1)} async-done(((bf16[8,64,256]{2,1,0:T(8,128)(2,1)}), bf16[8,64,256]{2,1,0:T(8,128)(2,1)}) %all-reduce.3.cloned.1.call-update) | async-done | bytes 262160 | tf_op jit(solution)/shard_map/while/body/eval_jaxpr/psum | solution.py:16
  906.6 16.0 dynamic_update_slice.8
  923.9 93.3 %all-reduce.3.cloned.1.call-done = bf16[8,64,256]{2,1,0:T(8,128)(2,1)} async-done(((bf16[8,64,256]{2,1,0:T(8,128)(2,1)}), bf16[8,64,256]{2,1,0:T(8,128)(2,1)}) %all-reduce.3.cloned.1.call-update) | async-done | bytes 262160 | tf_op jit(solution)/shard_map/while/body/eval_jaxpr/psum | solution.py:16
  1066.5 93.3 %all-reduce.3.cloned.1.call-done = bf16[8,64,256]{2,1,0:T(8,128)(2,1)} async-done(((bf16[8,64,256]{2,1,0:T(8,128)(2,1)}), bf16[8,64,256]{2,1,0:T(8,128)(2,1)}) %all-reduce.3.cloned.1.call-update) | async-done | bytes 262160 | tf_op jit(solution)/shard_map/while/body/eval_jaxpr/psum | solution.py:16
  1197.4 16.0 dynamic_update_slice.8
  1214.7 93.3 %all-reduce.3.cloned.1.call-done = bf16[8,64,256]{2,1,0:T(8,128)(2,1)} async-done(((bf16[8,64,256]{2,1,0:T(8,128)(2,1)}), bf16[8,64,256]{2,1,0:T(8,128)(2,1)}) %all-reduce.3.cloned.1.call-update) | async-done | bytes 262160 | tf_op jit(solution)/shard_map/while/body/eval_jaxpr/psum | solution.py:16
  1345.6 10.6 dynamic_update_slice.8
  1357.3 92.9 %all-reduce.3.cloned.1.call-done = bf16[8,64,256]{2,1,0:T(8,128)(2,1)} async-done(((bf16[8,64,256]{2,1,0:T(8,128)(2,1)}), bf16[8,64,256]{2,1,0:T(8,128)(2,1)}) %all-reduce.3.cloned.1.call-update) | async-done | bytes 262160 | tf_op jit(solution)/shard_map/while/body/eval_jaxpr/psum | solution.py:16
  1487.9 16.0 dynamic_update_slice.8
  1505.2 93.3 %all-reduce.3.cloned.1.call-done = bf16[8,64,256]{2,1,0:T(8,128)(2,1)} async-done(((bf16[8,64,256]{2,1,0:T(8,128)(2,1)}), bf16[8,64,256]{2,1,0:T(8,128)(2,1)}) %all-reduce.3.cloned.1.call-update) | async-done | bytes 262160 | tf_op jit(solution)/shard_map/while/body/eval_jaxpr/psum | solution.py:16
  1636.1 10.6 dynamic_update_slice.8
  1647.8 92.9 %all-reduce.3.cloned.1.call-done = bf16[8,64,256]{2,1,0:T(8,128)(2,1)} async-done(((bf16[8,64,256]{2,1,0:T(8,128)(2,1)}), bf16[8,64,256]{2,1,0:T(8,128)(2,1)}) %all-reduce.3.cloned.1.call-update) | async-done | bytes 262160 | tf_op jit(solution)/shard_map/while/body/eval_jaxpr/psum | solution.py:16
  1778.4 16.0 dynamic_update_slice.8
  1795.7 93.3 %all-reduce.3.cloned.1.call-done = bf16[8,64,256]{2,1,0:T(8,128)(2,1)} async-done(((bf16[8,64,256]{2,1,0:T(8,128)(2,1)}), bf16[8,64,256]{2,1,0:T(8,128)(2,1)}) %all-reduce.3.cloned.1.call-update) | async-done | bytes 262160 | tf_op jit(solution)/shard_map/while/body/eval_jaxpr/psum | solution.py:16
  1926.6 10.6 dynamic_update_slice.8
  1938.3 92.9 %all-reduce.3.cloned.1.call-done = bf16[8,64,256]{2,1,0:T(8,128)(2,1)} async-done(((bf16[8,64,256]{2,1,0:T(8,128)(2,1)}), bf16[8,64,256]{2,1,0:T(8,128)(2,1)}) %all-reduce.3.cloned.1.call-update) | async-done | bytes 262160 | tf_op jit(solution)/shard_map/while/body/eval_jaxpr/psum | solution.py:16
  2068.9 16.0 dynamic_update_slice.8
  2086.2 93.0 %all-reduce.3.cloned.1.call-done = bf16[8,64,256]{2,1,0:T(8,128)(2,1)} async-done(((bf16[8,64,256]{2,1,0:T(8,128)(2,1)}), bf16[8,64,256]{2,1,0:T(8,128)(2,1)}) %all-reduce.3.cloned.1.call-update) | async-done | bytes 262160 | tf_op jit(solution)/shard_map/while/body/eval_jaxpr/psum | solution.py:16
  2227.8 92.9 %all-reduce.3.cloned.1.call-done = bf16[8,64,256]{2,1,0:T(8,128)(2,1)} async-done(((bf16[8,64,256]{2,1,0:T(8,128)(2,1)}), bf16[8,64,256]{2,1,0:T(8,128)(2,1)}) %all-reduce.3.cloned.1.call-update) | async-done | bytes 262160 | tf_op jit(solution)/shard_map/while/body/eval_jaxpr/psum | solution.py:16
  2358.4 15.3 dynamic_update_slice.8
  (327 shorter events, 651.5 us)
Async XLA Ops:
  54.4 91.2 %all-reduce.3.cloned.1.call-start = ((), (), s32[]{:S(2)}) async-start(), calls=%async_computation | async-start | bytes 524288 | tf_op jit(solution)/shard_map/while/body/eval_jaxpr/psum | solution.py:16
  193.8 94.5 %all-reduce.3.cloned.1.call-start = ((), (), s32[]{:S(2)}) async-start(), calls=%async_computation | async-start | bytes 524288 | tf_op jit(solution)/shard_map/while/body/eval_jaxpr/psum | solution.py:16
  342.0 94.5 %all-reduce.3.cloned.1.call-start = ((), (), s32[]{:S(2)}) async-start(), calls=%async_computation | async-start | bytes 524288 | tf_op jit(solution)/shard_map/while/body/eval_jaxpr/psum | solution.py:16
  484.6 94.2 %all-reduce.3.cloned.1.call-start = ((), (), s32[]{:S(2)}) async-start(), calls=%async_computation | async-start | bytes 524288 | tf_op jit(solution)/shard_map/while/body/eval_jaxpr/psum | solution.py:16
  632.5 94.2 %all-reduce.3.cloned.1.call-start = ((), (), s32[]{:S(2)}) async-start(), calls=%async_computation | async-start | bytes 524288 | tf_op jit(solution)/shard_map/while/body/eval_jaxpr/psum | solution.py:16
  774.8 94.2 %all-reduce.3.cloned.1.call-start = ((), (), s32[]{:S(2)}) async-start(), calls=%async_computation | async-start | bytes 524288 | tf_op jit(solution)/shard_map/while/body/eval_jaxpr/psum | solution.py:16
  922.6 94.5 %all-reduce.3.cloned.1.call-start = ((), (), s32[]{:S(2)}) async-start(), calls=%async_computation | async-start | bytes 524288 | tf_op jit(solution)/shard_map/while/body/eval_jaxpr/psum | solution.py:16
  1065.3 94.5 %all-reduce.3.cloned.1.call-start = ((), (), s32[]{:S(2)}) async-start(), calls=%async_computation | async-start | bytes 524288 | tf_op jit(solution)/shard_map/while/body/eval_jaxpr/psum | solution.py:16
  1213.5 94.5 %all-reduce.3.cloned.1.call-start = ((), (), s32[]{:S(2)}) async-start(), calls=%async_computation | async-start | bytes 524288 | tf_op jit(solution)/shard_map/while/body/eval_jaxpr/psum | solution.py:16
  1356.1 94.2 %all-reduce.3.cloned.1.call-start = ((), (), s32[]{:S(2)}) async-start(), calls=%async_computation | async-start | bytes 524288 | tf_op jit(solution)/shard_map/while/body/eval_jaxpr/psum | solution.py:16
  1504.0 94.5 %all-reduce.3.cloned.1.call-start = ((), (), s32[]{:S(2)}) async-start(), calls=%async_computation | async-start | bytes 524288 | tf_op jit(solution)/shard_map/while/body/eval_jaxpr/psum | solution.py:16
  1646.6 94.2 %all-reduce.3.cloned.1.call-start = ((), (), s32[]{:S(2)}) async-start(), calls=%async_computation | async-start | bytes 524288 | tf_op jit(solution)/shard_map/while/body/eval_jaxpr/psum | solution.py:16
  1794.5 94.5 %all-reduce.3.cloned.1.call-start = ((), (), s32[]{:S(2)}) async-start(), calls=%async_computation | async-start | bytes 524288 | tf_op jit(solution)/shard_map/while/body/eval_jaxpr/psum | solution.py:16
  1937.1 94.2 %all-reduce.3.cloned.1.call-start = ((), (), s32[]{:S(2)}) async-start(), calls=%async_computation | async-start | bytes 524288 | tf_op jit(solution)/shard_map/while/body/eval_jaxpr/psum | solution.py:16
  2085.0 94.2 %all-reduce.3.cloned.1.call-start = ((), (), s32[]{:S(2)}) async-start(), calls=%async_computation | async-start | bytes 524288 | tf_op jit(solution)/shard_map/while/body/eval_jaxpr/psum | solution.py:16
  2226.6 94.2 %all-reduce.3.cloned.1.call-start = ((), (), s32[]{:S(2)}) async-start(), calls=%async_computation | async-start | bytes 524288 | tf_op jit(solution)/shard_map/while/body/eval_jaxpr/psum | solution.py:16
Sparse Core Ops, SparseCore 0:
  58.6 87.0 all-reduce.2
  198.0 90.2 all-reduce.2
  346.1 90.2 all-reduce.2
  488.5 90.2 all-reduce.2
  636.3 90.2 all-reduce.2
  778.7 90.2 all-reduce.2
  926.8 90.2 all-reduce.2
  1069.5 90.2 all-reduce.2
  1217.6 90.2 all-reduce.2
  1360.0 90.2 all-reduce.2
  1508.1 90.2 all-reduce.2
  1650.5 90.2 all-reduce.2
  1798.6 90.2 all-reduce.2
  1941.0 90.2 all-reduce.2
  2088.8 90.2 all-reduce.2
  2230.5 90.2 all-reduce.2
where the time goes:
time: 2390 us; the launch traced here: 2380 us
  waiting for transfers between devices  1490 us (62%)
  local copies, waits for them, and re-layouts  572 us (24%)
  matrix products  192 us (8%)
  other arithmetic  77.3 us (3%)
  blocking collectives  36.6 us (2%)
    psum x16, waiting for transfers between devices, spread(): return lax.psum(jnp.where(mine, value, jnp.zeros_like(value)), axis)  1490 us
    dot_general x64, local copies, waits for them, and re-layouts, product(): jnp.einsum('wif,wjf->ijf', left, right, preferred_element_type=jnp.float32)  327 us
    dynamic_update_slice x16, local copies, waits for them, and re-layouts, visit(): lax.dynamic_update_slice(current, block, (jnp.int32(0), jnp.int32(0), sta...  211 us
    dot_general x64, matrix products, product(): jnp.einsum('wif,wjf->ijf', left, right, preferred_element_type=jnp.float32)  174 us
    sub x16, other arithmetic, pair_block(): imag_sum = product(own_imag, other_real) - product(own_real, other_imag)  60.6 us
  transfers between devices with their start and end apart: 16, of which 16 were waited for; matrix products, arithmetic and copies ran while one was open for 0% of the time, Pallas kernels for 0%

commit v1 on v0

--- a/solution.py
+++ b/solution.py
@@ -13,7 +13,7 @@
 
 def spread(value, axis, root):
     mine = lax.axis_index(axis) == root
-    return lax.psum(jnp.where(mine, value, jnp.zeros_like(value)), axis)
+    return jnp.sum(lax.all_gather(jnp.where(mine, value, jnp.zeros_like(value)), axis), axis=0)
 
 
 def forward_table(width, bins):

time: 2390 us -> 1740 us (0.73)
  waiting for transfers between devices: 1490 us -> 810 us
  other arithmetic: 77.3 us -> 125 us
    psum x16 -> x0, waiting for transfers between devices: 1490 us -> none  [spread(): return lax.psum(jnp.where(mine, value, jnp.zeros_like(value)), axis)]
    all_gather x0 -> x16, waiting for transfers between devices: none -> 809 us  [spread(): lax.all_gather(jnp.where(mine, value, jnp.zeros_like(value)), axis)]
    reduce_sum x0 -> x16, other arithmetic: none -> 47.7 us  [spread(): jnp.sum(lax.all_gather(jnp.where(mine, value, jnp.zeros_like(value)), axi...]
where the time goes in v1:
time: 1740 us; the launch traced here: 1730 us
  waiting for transfers between devices  810 us (47%)
  local copies, waits for them, and re-layouts  556 us (32%)
  matrix products  192 us (11%)
  other arithmetic  125 us (7%)
  blocking collectives  36.6 us (2%)
    all_gather x16, waiting for transfers between devices, spread(): lax.all_gather(jnp.where(mine, value, jnp.zeros_like(value)), axis)  809 us
    dot_general x64, local copies, waits for them, and re-layouts, product(): jnp.einsum('wif,wjf->ijf', left, right, preferred_element_type=jnp.float32)  327 us
    dynamic_update_slice x16, local copies, waits for them, and re-layouts, visit(): lax.dynamic_update_slice(current, block, (jnp.int32(0), jnp.int32(0), sta...  211 us
    dot_general x64, matrix products, product(): jnp.einsum('wif,wjf->ijf', left, right, preferred_element_type=jnp.float32)  174 us
    sub x16, other arithmetic, pair_block(): imag_sum = product(own_imag, other_real) - product(own_real, other_imag)  60.6 us
    reduce_sum x16, other arithmetic, spread(): jnp.sum(lax.all_gather(jnp.where(mine, value, jnp.zeros_like(value)), axi...  47.7 us
    psum x1, blocking collectives, shards(): lax.psum((jnp.sum(traces * good[:, None], axis=0), jnp.sum(good)), 'chan')  36.6 us
  transfers between devices with their start and end apart: 16, of which 16 were waited for; matrix products, arithmetic and copies ran while one was open for 0% of the time, Pallas kernels for 0%

profile of v1, /device:TPU:0, one launch (start us, length us, event | category | flops | bytes accessed | tf_op | source)
XLA Modules:
  0.0 1734.5 jit_solution(2654132772915028153)
XLA Ops:
  9.5 36.6 %all-reduce = (f32[1152]{0:T(1024)S(1)}, f32[]{:T(128)}) all-reduce(f32[1152]{0:T(1024)S(1)} %multiply_reduce_fusion, f32[]{:T(128)} %convert_reduce_fusion), channel_id=1, replica_groups=mesh['groups'=2,'chan'=16] {'chan'}, use_global_device_ids=true, to_apply=%region_1.0 | all-reduce | flops 1153 | bytes 9224 | tf_op jit(solution)/shard_map/psum | solution.py:57
  54.7 1673.2 %while.15 = (s32[]{:T(128)}, bf16[64,64,1024]{2,1,0:T(8,128)(2,1)}, bf16[8,64,256]{1,0,2:T(8,128)(2,1)S(1)}, bf16[256,64]{0,1:T(8,128)(2,1)S(1)}, s32[]{:T(128)}...) while((s32[]{:T(128)}, bf16[64,64,1024]{2,1,0:T(8,128)(2,1)}, ...), condition=%wide.region_7.8_spmd, body=%wide.region_5.7_spmd.sunk | while | flops 174325760 | bytes 65568988 | solution.py:82
  55.8 49.5 %all-gather.5.cloned.1.call-done = bf16[128,64,256]{2,1,0:T(8,128)(2,1)} async-done(((bf16[8,64,256]{2,1,0:T(8,128)(2,1)}), bf16[128,64,256]{2,1,0:T(8,128)(2,1)}) %all-gather.5.cloned.1.call-update) | async-done | bytes 4194320 | tf_op jit(solution)/shard_map/while/body/eval_jaxpr/all_gather | solution.py:16
  145.0 10.6 dynamic_update_slice.11
  156.7 50.8 %all-gather.5.cloned.1.call-done = bf16[128,64,256]{2,1,0:T(8,128)(2,1)} async-done(((bf16[8,64,256]{2,1,0:T(8,128)(2,1)}), bf16[128,64,256]{2,1,0:T(8,128)(2,1)}) %all-gather.5.cloned.1.call-update) | async-done | bytes 4194320 | tf_op jit(solution)/shard_map/while/body/eval_jaxpr/all_gather | solution.py:16
  247.2 16.0 dynamic_update_slice.11
  264.3 50.8 %all-gather.5.cloned.1.call-done = bf16[128,64,256]{2,1,0:T(8,128)(2,1)} async-done(((bf16[8,64,256]{2,1,0:T(8,128)(2,1)}), bf16[128,64,256]{2,1,0:T(8,128)(2,1)}) %all-gather.5.cloned.1.call-update) | async-done | bytes 4194320 | tf_op jit(solution)/shard_map/while/body/eval_jaxpr/all_gather | solution.py:16
  354.8 10.6 dynamic_update_slice.11
  366.5 50.5 %all-gather.5.cloned.1.call-done = bf16[128,64,256]{2,1,0:T(8,128)(2,1)} async-done(((bf16[8,64,256]{2,1,0:T(8,128)(2,1)}), bf16[128,64,256]{2,1,0:T(8,128)(2,1)}) %all-gather.5.cloned.1.call-update) | async-done | bytes 4194320 | tf_op jit(solution)/shard_map/while/body/eval_jaxpr/all_gather | solution.py:16
  456.7 16.0 dynamic_update_slice.11
  473.8 50.5 %all-gather.5.cloned.1.call-done = bf16[128,64,256]{2,1,0:T(8,128)(2,1)} async-done(((bf16[8,64,256]{2,1,0:T(8,128)(2,1)}), bf16[128,64,256]{2,1,0:T(8,128)(2,1)}) %all-gather.5.cloned.1.call-update) | async-done | bytes 4194320 | tf_op jit(solution)/shard_map/while/body/eval_jaxpr/all_gather | solution.py:16
  564.0 10.6 dynamic_update_slice.11
  575.7 50.5 %all-gather.5.cloned.1.call-done = bf16[128,64,256]{2,1,0:T(8,128)(2,1)} async-done(((bf16[8,64,256]{2,1,0:T(8,128)(2,1)}), bf16[128,64,256]{2,1,0:T(8,128)(2,1)}) %all-gather.5.cloned.1.call-update) | async-done | bytes 4194320 | tf_op jit(solution)/shard_map/while/body/eval_jaxpr/all_gather | solution.py:16
  665.9 16.0 dynamic_update_slice.11
  683.0 50.8 %all-gather.5.cloned.1.call-done = bf16[128,64,256]{2,1,0:T(8,128)(2,1)} async-done(((bf16[8,64,256]{2,1,0:T(8,128)(2,1)}), bf16[128,64,256]{2,1,0:T(8,128)(2,1)}) %all-gather.5.cloned.1.call-update) | async-done | bytes 4194320 | tf_op jit(solution)/shard_map/while/body/eval_jaxpr/all_gather | solution.py:16
  773.5 10.6 dynamic_update_slice.11
  785.1 50.8 %all-gather.5.cloned.1.call-done = bf16[128,64,256]{2,1,0:T(8,128)(2,1)} async-done(((bf16[8,64,256]{2,1,0:T(8,128)(2,1)}), bf16[128,64,256]{2,1,0:T(8,128)(2,1)}) %all-gather.5.cloned.1.call-update) | async-done | bytes 4194320 | tf_op jit(solution)/shard_map/while/body/eval_jaxpr/all_gather | solution.py:16
  875.7 16.0 dynamic_update_slice.11
  892.8 50.8 %all-gather.5.cloned.1.call-done = bf16[128,64,256]{2,1,0:T(8,128)(2,1)} async-done(((bf16[8,64,256]{2,1,0:T(8,128)(2,1)}), bf16[128,64,256]{2,1,0:T(8,128)(2,1)}) %all-gather.5.cloned.1.call-update) | async-done | bytes 4194320 | tf_op jit(solution)/shard_map/while/body/eval_jaxpr/all_gather | solution.py:16
  983.3 10.6 dynamic_update_slice.11
  995.0 50.5 %all-gather.5.cloned.1.call-done = bf16[128,64,256]{2,1,0:T(8,128)(2,1)} async-done(((bf16[8,64,256]{2,1,0:T(8,128)(2,1)}), bf16[128,64,256]{2,1,0:T(8,128)(2,1)}) %all-gather.5.cloned.1.call-update) | async-done | bytes 4194320 | tf_op jit(solution)/shard_map/while/body/eval_jaxpr/all_gather | solution.py:16
  1085.2 16.0 dynamic_update_slice.11
  1102.3 50.8 %all-gather.5.cloned.1.call-done = bf16[128,64,256]{2,1,0:T(8,128)(2,1)} async-done(((bf16[8,64,256]{2,1,0:T(8,128)(2,1)}), bf16[128,64,256]{2,1,0:T(8,128)(2,1)}) %all-gather.5.cloned.1.call-update) | async-done | bytes 4194320 | tf_op jit(solution)/shard_map/while/body/eval_jaxpr/all_gather | solution.py:16
  1204.5 50.5 %all-gather.5.cloned.1.call-done = bf16[128,64,256]{2,1,0:T(8,128)(2,1)} async-done(((bf16[8,64,256]{2,1,0:T(8,128)(2,1)}), bf16[128,64,256]{2,1,0:T(8,128)(2,1)}) %all-gather.5.cloned.1.call-update) | async-done | bytes 4194320 | tf_op jit(solution)/shard_map/while/body/eval_jaxpr/all_gather | solution.py:16
  1294.7 16.0 dynamic_update_slice.11
  1311.8 50.8 %all-gather.5.cloned.1.call-done = bf16[128,64,256]{2,1,0:T(8,128)(2,1)} async-done(((bf16[8,64,256]{2,1,0:T(8,128)(2,1)}), bf16[128,64,256]{2,1,0:T(8,128)(2,1)}) %all-gather.5.cloned.1.call-update) | async-done | bytes 4194320 | tf_op jit(solution)/shard_map/while/body/eval_jaxpr/all_gather | solution.py:16
  1402.3 10.6 dynamic_update_slice.11
  1413.9 50.5 %all-gather.5.cloned.1.call-done = bf16[128,64,256]{2,1,0:T(8,128)(2,1)} async-done(((bf16[8,64,256]{2,1,0:T(8,128)(2,1)}), bf16[128,64,256]{2,1,0:T(8,128)(2,1)}) %all-gather.5.cloned.1.call-update) | async-done | bytes 4194320 | tf_op jit(solution)/shard_map/while/body/eval_jaxpr/all_gather | solution.py:16
  1504.2 16.0 dynamic_update_slice.11
  1521.3 50.5 %all-gather.5.cloned.1.call-done = bf16[128,64,256]{2,1,0:T(8,128)(2,1)} async-done(((bf16[8,64,256]{2,1,0:T(8,128)(2,1)}), bf16[128,64,256]{2,1,0:T(8,128)(2,1)}) %all-gather.5.cloned.1.call-update) | async-done | bytes 4194320 | tf_op jit(solution)/shard_map/while/body/eval_jaxpr/all_gather | solution.py:16
  1622.4 50.5 %all-gather.5.cloned.1.call-done = bf16[128,64,256]{2,1,0:T(8,128)(2,1)} async-done(((bf16[8,64,256]{2,1,0:T(8,128)(2,1)}), bf16[128,64,256]{2,1,0:T(8,128)(2,1)}) %all-gather.5.cloned.1.call-update) | async-done | bytes 4194320 | tf_op jit(solution)/shard_map/while/body/eval_jaxpr/all_gather | solution.py:16
  1712.6 15.3 dynamic_update_slice.11
  (312 shorter events, 682.6 us)
Async XLA Ops:
  54.7 50.6 %all-gather.5.cloned.1.call-start = ((), (), s32[]{:S(2)}) async-start(), calls=%async_computation | async-start | bytes 4456448 | tf_op jit(solution)/shard_map/while/body/eval_jaxpr/all_gather | solution.py:16
  155.6 51.9 %all-gather.5.cloned.1.call-start = ((), (), s32[]{:S(2)}) async-start(), calls=%async_computation | async-start | bytes 4456448 | tf_op jit(solution)/shard_map/while/body/eval_jaxpr/all_gather | solution.py:16
  263.2 51.9 %all-gather.5.cloned.1.call-start = ((), (), s32[]{:S(2)}) async-start(), calls=%async_computation | async-start | bytes 4456448 | tf_op jit(solution)/shard_map/while/body/eval_jaxpr/all_gather | solution.py:16
  365.4 51.6 %all-gather.5.cloned.1.call-start = ((), (), s32[]{:S(2)}) async-start(), calls=%async_computation | async-start | bytes 4456448 | tf_op jit(solution)/shard_map/while/body/eval_jaxpr/all_gather | solution.py:16
  472.7 51.6 %all-gather.5.cloned.1.call-start = ((), (), s32[]{:S(2)}) async-start(), calls=%async_computation | async-start | bytes 4456448 | tf_op jit(solution)/shard_map/while/body/eval_jaxpr/all_gather | solution.py:16
  574.6 51.6 %all-gather.5.cloned.1.call-start = ((), (), s32[]{:S(2)}) async-start(), calls=%async_computation | async-start | bytes 4456448 | tf_op jit(solution)/shard_map/while/body/eval_jaxpr/all_gather | solution.py:16
  681.9 51.9 %all-gather.5.cloned.1.call-start = ((), (), s32[]{:S(2)}) async-start(), calls=%async_computation | async-start | bytes 4456448 | tf_op jit(solution)/shard_map/while/body/eval_jaxpr/all_gather | solution.py:16
  784.1 51.9 %all-gather.5.cloned.1.call-start = ((), (), s32[]{:S(2)}) async-start(), calls=%async_computation | async-start | bytes 4456448 | tf_op jit(solution)/shard_map/while/body/eval_jaxpr/all_gather | solution.py:16
  891.7 51.9 %all-gather.5.cloned.1.call-start = ((), (), s32[]{:S(2)}) async-start(), calls=%async_computation | async-start | bytes 4456448 | tf_op jit(solution)/shard_map/while/body/eval_jaxpr/all_gather | solution.py:16
  993.9 51.6 %all-gather.5.cloned.1.call-start = ((), (), s32[]{:S(2)}) async-start(), calls=%async_computation | async-start | bytes 4456448 | tf_op jit(solution)/shard_map/while/body/eval_jaxpr/all_gather | solution.py:16
  1101.2 51.9 %all-gather.5.cloned.1.call-start = ((), (), s32[]{:S(2)}) async-start(), calls=%async_computation | async-start | bytes 4456448 | tf_op jit(solution)/shard_map/while/body/eval_jaxpr/all_gather | solution.py:16
  1203.4 51.6 %all-gather.5.cloned.1.call-start = ((), (), s32[]{:S(2)}) async-start(), calls=%async_computation | async-start | bytes 4456448 | tf_op jit(solution)/shard_map/while/body/eval_jaxpr/all_gather | solution.py:16
  1310.7 51.9 %all-gather.5.cloned.1.call-start = ((), (), s32[]{:S(2)}) async-start(), calls=%async_computation | async-start | bytes 4456448 | tf_op jit(solution)/shard_map/while/body/eval_jaxpr/all_gather | solution.py:16
  1412.9 51.6 %all-gather.5.cloned.1.call-start = ((), (), s32[]{:S(2)}) async-start(), calls=%async_computation | async-start | bytes 4456448 | tf_op jit(solution)/shard_map/while/body/eval_jaxpr/all_gather | solution.py:16
  1520.2 51.6 %all-gather.5.cloned.1.call-start = ((), (), s32[]{:S(2)}) async-start(), calls=%async_computation | async-start | bytes 4456448 | tf_op jit(solution)/shard_map/while/body/eval_jaxpr/all_gather | solution.py:16
  1621.3 51.6 %all-gather.5.cloned.1.call-start = ((), (), s32[]{:S(2)}) async-start(), calls=%async_computation | async-start | bytes 4456448 | tf_op jit(solution)/shard_map/while/body/eval_jaxpr/all_gather | solution.py:16
Sparse Core Ops, SparseCore 0:
  57.7 47.6 all-gather.4
  158.5 48.9 all-gather.4
  266.2 48.8 all-gather.4
  368.0 48.8 all-gather.4
  475.4 48.8 all-gather.4
  577.2 48.8 all-gather.4
  684.9 48.8 all-gather.4
  787.0 48.9 all-gather.4
  894.7 48.8 all-gather.4
  996.5 48.8 all-gather.4
  1104.2 48.8 all-gather.4
  1206.0 48.8 all-gather.4
  1313.7 48.8 all-gather.4
  1415.5 48.9 all-gather.4
  1522.8 48.8 all-gather.4
  1624.0 48.8 all-gather.4
